TPU v7x, 32 devices: a whole 2x2x4 slice. The times are simulated.
32 devices in a mesh: grid: 8 (over z, x), mem: 4 (over y, core).
Axes of the slice: x: 2, y: 2, z: 4, core: 2. Of those that a mesh axis runs over, the one named last changes fastest.
Arguments:
- members: bfloat16 [80, 4, 16, 512], P('mem', None, 'grid'), may hold values from -0.8984375 to 0.8984375
- innovation: float32 [4, 16, 512], P(None, 'grid'), may hold values from -6 to 6
- observed_count: int32 [16, 512], P('grid'), may hold values from 0 to 3
- obs_precision: float32 [4], replicated, may hold values from 0.5 to 4
Outputs:
- recentred: bfloat16 [80, 4, 16, 512], P('mem', None, 'grid')
- increment: float32 [4, 16, 512], P('mem', 'grid')
All inputs are finite; a program needn't handle non-finite values.
Results may differ from a plain program's by a relative error of at most 0.0004.
Values may be sent and summed in bfloat16 or wider, within the bound.
No kernel may reach another device: no remote copies, remote signals or barrier semaphores. Data moves between devices by JAX's collectives and lax.ppermute only.
A program may use at most 64 MiB of HBM per device.

v0:
```python
import jax
import jax.numpy as jnp
from jax import lax
from jax.sharding import PartitionSpec as P

PASSES = 2
ITERS = 2
diffusion = 0.25


def padded(value, sides, width):
    for axis, dim in sides:
        devices, length = (lax.axis_size(axis), value.shape[dim])
        up = [(i, (i + 1) % devices) for i in range(devices - 1)]
        down = [(j, i) for i, j in up]
        last = lax.slice_in_dim(value, length - width, length, axis=dim)
        leading = lax.slice_in_dim(value, 0, width, axis=dim)
        before = lax.ppermute(last, axis, up)
        after = lax.ppermute(leading, axis, down)
        value = jnp.concatenate([before, value, after], axis=dim)
    return value


def smooth(field):
    for sweep_index in range(PASSES):
        extended = padded(field, (("grid", 2),), 1)
        centre = extended[:, :, 1:-1]
        field = centre + diffusion * (extended[:, :, :-2] + extended[:, :, 2:] - 2.0 * centre)
    for sweep_index in range(PASSES):
        field = field + diffusion * (jnp.roll(field, 1, 3) + jnp.roll(field, -1, 3) - 2.0 * field)
    return field


def member_total(product):
    summed = jnp.sum(product, axis=0)
    return summed


def norm_of(residual):
    return lax.psum(jnp.sum(residual * residual), ("grid", "mem"))


def local(members, innovation, observed_count, obs_precision):
    mem_index = lax.axis_index("mem")
    level_share = members.shape[1] // lax.axis_size("mem")
    perturbed = lax.all_to_all(members, "mem", split_axis=1, concat_axis=0, tiled=True)
    precision = lax.dynamic_slice_in_dim(obs_precision, mem_index * level_share, level_share, 0)
    local_innovation = lax.dynamic_slice_in_dim(innovation, mem_index * level_share, level_share, 0)
    weight = observed_count.astype(jnp.float32)[None] * precision[:, None, None]
    gradient = smooth(perturbed * (weight * local_innovation)[None])
    carried = jnp.zeros_like(gradient)
    residual = gradient
    direction = residual
    norm_now = norm_of(residual)
    for iteration in range(ITERS):
        smoothed = smooth(direction)
        total = member_total(perturbed * smoothed)
        back = smooth(perturbed * (weight * total)[None])
        image, smoothed = (direction + back, smoothed)
        step_size = norm_now / lax.psum(jnp.sum(direction * image), ("grid", "mem"))
        carried = carried + step_size * smoothed
        residual = residual - step_size * image
        if iteration + 1 < ITERS:
            norm_next = norm_of(residual)
            direction = residual + norm_next / norm_now * direction
            norm_now = norm_next
    increment = member_total(perturbed * carried)
    whole = lax.all_gather(increment, "mem", axis=0, tiled=True)
    recentred = (members.astype(jnp.float32) + whole[None]).astype(jnp.bfloat16)
    return (recentred, increment)


def solution(mesh):
    placed = (P("mem", None, "grid", None), P(None, "grid", None), P("grid", None), P())
    return jax.shard_map(
        local,
        mesh=mesh,
        in_specs=placed,
        out_specs=(P("mem", None, "grid", None), P("mem", "grid", None)),
        check_vma=False,
    )
```

profile of v0, /device:TPU:0, one launch (start us, length us, event | category | flops | bytes accessed | tf_op | source)
XLA Modules:
  0.0 294.0 jit_solution(12753605812569267372)
XLA Ops:
  2.3 4.3 %all-to-all-start = ((bf16[20,4,2,512]{3,2,0,1:T(2,128)(2,1)}), bf16[20,4,2,512]{3,2,0,1:T(2,128)(2,1)S(1)}, u32[]{:S(2)}, u32[]{:S(2)}) async-start(bf16[20,4,2,512]{3,2,0,1:T(2,128)(2,1)} %copy.7), calls=%async_computation | async-start | bytes 327680 | tf_op jit(solution)/shard_map/all_to_all | solution.py:46
  12.0 3.9 %collective-permute-start = (f32[80,1,1,512]{3,2,0,1:T(1,128)S(1)}, f32[80,1,1,512]{3,2,0,1:T(1,128)S(1)}, u32[]{:S(2)}, u32[]{:S(2)}) collective-permute-start(f32[80,1,1,512]{3,2,0,1:T(1,128)S(1)} %get-tuple-element.69), channel_id=1, source_target_pairs={{0,4},{4,8},{8,12},{12,16},{16,20},{20,24},{24,28},{1,5},{5,9},{9,... | collective-permute-start | bytes 491528 | tf_op jit(solution)/shard_map/ppermute | solution.py:18
  18.9 4.2 %collective-permute-done.1 = f32[80,1,1,512]{3,2,0,1:T(1,128)S(1)} collective-permute-done((f32[80,1,1,512]{3,2,0,1:T(1,128)S(1)}, f32[80,1,1,512]{3,2,0,1:T(1,128)S(1)}, u32[]{:S(2)}, u32[]{:S(2)}) %collective-permute-start.1) | collective-permute-done | bytes 163872 | tf_op jit(solution)/shard_map/ppermute | solution.py:19
  24.1 4.4 %collective-permute-start.2 = (f32[80,1,1,512]{3,2,0,1:T(1,128)S(1)}, f32[80,1,1,512]{3,2,0,1:T(1,128)S(1)}, u32[]{:S(2)}, u32[]{:S(2)}) collective-permute-start(f32[80,1,1,512]{3,2,0,1:T(1,128)S(1)} %get-tuple-element.67), channel_id=1, source_target_pairs={{0,4},{4,8},{8,12},{12,16},{16,20},{20,24},{24,28},{1,5},{5,9},{9,... | collective-permute-start | bytes 491528 | tf_op jit(solution)/shard_map/ppermute | solution.py:18
  31.3 4.5 %collective-permute-done.3 = f32[80,1,1,512]{3,2,0,1:T(1,128)S(1)} collective-permute-done((f32[80,1,1,512]{3,2,0,1:T(1,128)S(1)}, f32[80,1,1,512]{3,2,0,1:T(1,128)S(1)}, u32[]{:S(2)}, u32[]{:S(2)}) %collective-permute-start.3) | collective-permute-done | bytes 163872 | tf_op jit(solution)/shard_map/ppermute | solution.py:19
  39.7 4.5 %collective-permute-start.4 = (f32[80,1,1,512]{3,2,0,1:T(1,128)S(1)}, f32[80,1,1,512]{3,2,0,1:T(1,128)S(1)}, u32[]{:S(2)}, u32[]{:S(2)}) collective-permute-start(f32[80,1,1,512]{3,2,0,1:T(1,128)S(1)} %get-tuple-element.57), channel_id=1, source_target_pairs={{0,4},{4,8},{8,12},{12,16},{16,20},{20,24},{24,28},{1,5},{5,9},{9,... | collective-permute-start | bytes 491528 | tf_op jit(solution)/shard_map/ppermute | solution.py:18
  47.1 4.9 %collective-permute-done.5 = f32[80,1,1,512]{3,2,0,1:T(1,128)S(1)} collective-permute-done((f32[80,1,1,512]{3,2,0,1:T(1,128)S(1)}, f32[80,1,1,512]{3,2,0,1:T(1,128)S(1)}, u32[]{:S(2)}, u32[]{:S(2)}) %collective-permute-start.5) | collective-permute-done | bytes 163872 | tf_op jit(solution)/shard_map/ppermute | solution.py:19
  53.0 4.5 %collective-permute-start.6 = (f32[80,1,1,512]{3,2,0,1:T(1,128)S(1)}, f32[80,1,1,512]{3,2,0,1:T(1,128)S(1)}, u32[]{:S(2)}, u32[]{:S(2)}) collective-permute-start(f32[80,1,1,512]{3,2,0,1:T(1,128)S(1)} %get-tuple-element.55), channel_id=1, source_target_pairs={{0,4},{4,8},{8,12},{12,16},{16,20},{20,24},{24,28},{1,5},{5,9},{9,... | collective-permute-start | bytes 491528 | tf_op jit(solution)/shard_map/ppermute | solution.py:18
  60.3 5.1 %collective-permute-done.7 = f32[80,1,1,512]{3,2,0,1:T(1,128)S(1)} collective-permute-done((f32[80,1,1,512]{3,2,0,1:T(1,128)S(1)}, f32[80,1,1,512]{3,2,0,1:T(1,128)S(1)}, u32[]{:S(2)}, u32[]{:S(2)}) %collective-permute-start.7) | collective-permute-done | bytes 163872 | tf_op jit(solution)/shard_map/ppermute | solution.py:19
  70.1 4.5 %collective-permute-start.8 = (f32[80,1,1,512]{3,2,0,1:T(1,128)S(1)}, f32[80,1,1,512]{3,2,0,1:T(1,128)S(1)}, u32[]{:S(2)}, u32[]{:S(2)}) collective-permute-start(f32[80,1,1,512]{3,2,0,1:T(1,128)S(1)} %get-tuple-element.45), channel_id=1, source_target_pairs={{0,4},{4,8},{8,12},{12,16},{16,20},{20,24},{24,28},{1,5},{5,9},{9,... | collective-permute-start | bytes 491528 | tf_op jit(solution)/shard_map/ppermute | solution.py:18
  77.5 5.1 %collective-permute-done.9 = f32[80,1,1,512]{3,2,0,1:T(1,128)S(1)} collective-permute-done((f32[80,1,1,512]{3,2,0,1:T(1,128)S(1)}, f32[80,1,1,512]{3,2,0,1:T(1,128)S(1)}, u32[]{:S(2)}, u32[]{:S(2)}) %collective-permute-start.9) | collective-permute-done | bytes 163872 | tf_op jit(solution)/shard_map/ppermute | solution.py:19
  83.5 4.5 %collective-permute-start.10 = (f32[80,1,1,512]{3,2,0,1:T(1,128)S(1)}, f32[80,1,1,512]{3,2,0,1:T(1,128)S(1)}, u32[]{:S(2)}, u32[]{:S(2)}) collective-permute-start(f32[80,1,1,512]{3,2,0,1:T(1,128)S(1)} %get-tuple-element.43), channel_id=1, source_target_pairs={{0,4},{4,8},{8,12},{12,16},{16,20},{20,24},{24,28},{1,5},{5,9},{9,... | collective-permute-start | bytes 491528 | tf_op jit(solution)/shard_map/ppermute | solution.py:18
  90.9 5.1 %collective-permute-done.11 = f32[80,1,1,512]{3,2,0,1:T(1,128)S(1)} collective-permute-done((f32[80,1,1,512]{3,2,0,1:T(1,128)S(1)}, f32[80,1,1,512]{3,2,0,1:T(1,128)S(1)}, u32[]{:S(2)}, u32[]{:S(2)}) %collective-permute-start.11) | collective-permute-done | bytes 163872 | tf_op jit(solution)/shard_map/ppermute | solution.py:19
  100.5 41.8 %all-reduce = (f32[]{:T(128)}, f32[]{:T(128)}) all-reduce(f32[]{:T(128)} %get-tuple-element.3, f32[]{:T(128)} %get-tuple-element.2), channel_id=1, replica_groups=mesh['grid'=8,'mem'=4] {'grid','mem'}, use_global_device_ids=true, to_apply=%region_1.2 | all-reduce | flops 2 | bytes 16 | tf_op jit(solution)/shard_map/psum | solution.py:40
  144.6 40.8 %psum.30 = f32[]{:T(128)} all-reduce(f32[]{:T(128)} %multiply_reduce_fusion.2), channel_id=1, replica_groups=mesh['grid'=8,'mem'=4] {'grid','mem'}, use_global_device_ids=true, to_apply=%region_6.7 | all-reduce | flops 1 | bytes 8 | tf_op jit(solution)/shard_map/psum | solution.py:40
  187.2 4.2 %collective-permute-start.12 = (f32[80,1,1,512]{3,2,0,1:T(1,128)S(1)}, f32[80,1,1,512]{3,2,0,1:T(1,128)S(1)}, u32[]{:S(2)}, u32[]{:S(2)}) collective-permute-start(f32[80,1,1,512]{3,2,0,1:T(1,128)S(1)} %get-tuple-element.33), channel_id=1, source_target_pairs={{0,4},{4,8},{8,12},{12,16},{16,20},{20,24},{24,28},{1,5},{5,9},{9,... | collective-permute-start | bytes 491528 | tf_op jit(solution)/shard_map/ppermute | solution.py:18
  192.7 5.1 %collective-permute-done.12 = f32[80,1,1,512]{3,2,0,1:T(1,128)S(1)} collective-permute-done((f32[80,1,1,512]{3,2,0,1:T(1,128)S(1)}, f32[80,1,1,512]{3,2,0,1:T(1,128)S(1)}, u32[]{:S(2)}, u32[]{:S(2)}) %collective-permute-start.12) | collective-permute-done | bytes 163872 | tf_op jit(solution)/shard_map/ppermute | solution.py:18
  206.0 4.4 %collective-permute-done.15 = f32[80,1,1,512]{3,2,0,1:T(1,128)S(1)} collective-permute-done((f32[80,1,1,512]{3,2,0,1:T(1,128)S(1)}, f32[80,1,1,512]{3,2,0,1:T(1,128)S(1)}, u32[]{:S(2)}, u32[]{:S(2)}) %collective-permute-start.15) | collective-permute-done | bytes 163872 | tf_op jit(solution)/shard_map/ppermute | solution.py:19
  215.0 3.7 %collective-permute-start.16 = (f32[80,1,1,512]{3,2,0,1:T(1,128)S(1)}, f32[80,1,1,512]{3,2,0,1:T(1,128)S(1)}, u32[]{:S(2)}, u32[]{:S(2)}) collective-permute-start(f32[80,1,1,512]{3,2,0,1:T(1,128)S(1)} %get-tuple-element.21), channel_id=1, source_target_pairs={{0,4},{4,8},{8,12},{12,16},{16,20},{20,24},{24,28},{1,5},{5,9},{9,... | collective-permute-start | bytes 491528 | tf_op jit(solution)/shard_map/ppermute | solution.py:18
  221.6 4.4 %collective-permute-done.17 = f32[80,1,1,512]{3,2,0,1:T(1,128)S(1)} collective-permute-done((f32[80,1,1,512]{3,2,0,1:T(1,128)S(1)}, f32[80,1,1,512]{3,2,0,1:T(1,128)S(1)}, u32[]{:S(2)}, u32[]{:S(2)}) %collective-permute-start.17) | collective-permute-done | bytes 163872 | tf_op jit(solution)/shard_map/ppermute | solution.py:19
  227.0 4.4 %collective-permute-start.18 = (f32[80,1,1,512]{3,2,0,1:T(1,128)S(1)}, f32[80,1,1,512]{3,2,0,1:T(1,128)S(1)}, u32[]{:S(2)}, u32[]{:S(2)}) collective-permute-start(f32[80,1,1,512]{3,2,0,1:T(1,128)S(1)} %get-tuple-element.19), channel_id=1, source_target_pairs={{0,4},{4,8},{8,12},{12,16},{16,20},{20,24},{24,28},{1,5},{5,9},{9,... | collective-permute-start | bytes 491528 | tf_op jit(solution)/shard_map/ppermute | solution.py:18
  234.2 5.1 %collective-permute-done.19 = f32[80,1,1,512]{3,2,0,1:T(1,128)S(1)} collective-permute-done((f32[80,1,1,512]{3,2,0,1:T(1,128)S(1)}, f32[80,1,1,512]{3,2,0,1:T(1,128)S(1)}, u32[]{:S(2)}, u32[]{:S(2)}) %collective-permute-start.19) | collective-permute-done | bytes 163872 | tf_op jit(solution)/shard_map/ppermute | solution.py:19
  243.6 42.2 %psum.31 = f32[]{:T(128)} all-reduce(f32[]{:T(128)} %fusion), channel_id=1, replica_groups=mesh['grid'=8,'mem'=4] {'grid','mem'}, use_global_device_ids=true, to_apply=%region_9.10 | all-reduce | flops 1 | bytes 8 | tf_op jit(solution)/shard_map/psum | solution.py:60
  287.4 5.7 %all-gather.1 = f32[4,2,512]{2,1,0:T(2,128)S(1)} all-gather(f32[1,2,512]{2,1,0:T(2,128)S(1)} %bitcast.46), channel_id=2, replica_groups=mesh['grid'=8,'mem'=4] {'mem'}, dimensions={0}, use_global_device_ids=true | all-gather | bytes 20480 | tf_op jit(solution)/shard_map/all_gather | solution.py:68
  (96 shorter events, 67.5 us)
Async XLA Ops:
  2.3 9.2 %all-to-all-start = ((bf16[20,4,2,512]{3,2,0,1:T(2,128)(2,1)}), bf16[20,4,2,512]{3,2,0,1:T(2,128)(2,1)S(1)}, u32[]{:S(2)}, u32[]{:S(2)}) async-start(bf16[20,4,2,512]{3,2,0,1:T(2,128)(2,1)} %copy.7), calls=%async_computation | async-start | bytes 327680 | tf_op jit(solution)/shard_map/all_to_all | solution.py:46
  6.6 1.2 copy-start.1
  12.0 6.9 %collective-permute-start = (f32[80,1,1,512]{3,2,0,1:T(1,128)S(1)}, f32[80,1,1,512]{3,2,0,1:T(1,128)S(1)}, u32[]{:S(2)}, u32[]{:S(2)}) collective-permute-start(f32[80,1,1,512]{3,2,0,1:T(1,128)S(1)} %get-tuple-element.69), channel_id=1, source_target_pairs={{0,4},{4,8},{8,12},{12,16},{16,20},{20,24},{24,28},{1,5},{5,9},{9,... | collective-permute-start | bytes 491528 | tf_op jit(solution)/shard_map/ppermute | solution.py:18
  15.9 7.2 %collective-permute-start.1 = (f32[80,1,1,512]{3,2,0,1:T(1,128)S(1)}, f32[80,1,1,512]{3,2,0,1:T(1,128)S(1)}, u32[]{:S(2)}, u32[]{:S(2)}) collective-permute-start(f32[80,1,1,512]{3,2,0,1:T(1,128)S(1)} %get-tuple-element.70), channel_id=1, source_target_pairs={{4,0},{8,4},{12,8},{16,12},{20,16},{24,20},{28,24},{5,1},{9,5},{13... | collective-permute-start | bytes 491528 | tf_op jit(solution)/shard_map/ppermute | solution.py:19
  24.1 7.2 %collective-permute-start.2 = (f32[80,1,1,512]{3,2,0,1:T(1,128)S(1)}, f32[80,1,1,512]{3,2,0,1:T(1,128)S(1)}, u32[]{:S(2)}, u32[]{:S(2)}) collective-permute-start(f32[80,1,1,512]{3,2,0,1:T(1,128)S(1)} %get-tuple-element.67), channel_id=1, source_target_pairs={{0,4},{4,8},{8,12},{12,16},{16,20},{20,24},{24,28},{1,5},{5,9},{9,... | collective-permute-start | bytes 491528 | tf_op jit(solution)/shard_map/ppermute | solution.py:18
  28.5 7.3 %collective-permute-start.3 = (f32[80,1,1,512]{3,2,0,1:T(1,128)S(1)}, f32[80,1,1,512]{3,2,0,1:T(1,128)S(1)}, u32[]{:S(2)}, u32[]{:S(2)}) collective-permute-start(f32[80,1,1,512]{3,2,0,1:T(1,128)S(1)} %get-tuple-element.68), channel_id=1, source_target_pairs={{4,0},{8,4},{12,8},{16,12},{20,16},{24,20},{28,24},{5,1},{9,5},{13... | collective-permute-start | bytes 491528 | tf_op jit(solution)/shard_map/ppermute | solution.py:19
  39.7 7.4 %collective-permute-start.4 = (f32[80,1,1,512]{3,2,0,1:T(1,128)S(1)}, f32[80,1,1,512]{3,2,0,1:T(1,128)S(1)}, u32[]{:S(2)}, u32[]{:S(2)}) collective-permute-start(f32[80,1,1,512]{3,2,0,1:T(1,128)S(1)} %get-tuple-element.57), channel_id=1, source_target_pairs={{0,4},{4,8},{8,12},{12,16},{16,20},{20,24},{24,28},{1,5},{5,9},{9,... | collective-permute-start | bytes 491528 | tf_op jit(solution)/shard_map/ppermute | solution.py:18
  44.2 7.7 %collective-permute-start.5 = (f32[80,1,1,512]{3,2,0,1:T(1,128)S(1)}, f32[80,1,1,512]{3,2,0,1:T(1,128)S(1)}, u32[]{:S(2)}, u32[]{:S(2)}) collective-permute-start(f32[80,1,1,512]{3,2,0,1:T(1,128)S(1)} %get-tuple-element.58), channel_id=1, source_target_pairs={{4,0},{8,4},{12,8},{16,12},{20,16},{24,20},{28,24},{5,1},{9,5},{13... | collective-permute-start | bytes 491528 | tf_op jit(solution)/shard_map/ppermute | solution.py:19
  53.0 7.4 %collective-permute-start.6 = (f32[80,1,1,512]{3,2,0,1:T(1,128)S(1)}, f32[80,1,1,512]{3,2,0,1:T(1,128)S(1)}, u32[]{:S(2)}, u32[]{:S(2)}) collective-permute-start(f32[80,1,1,512]{3,2,0,1:T(1,128)S(1)} %get-tuple-element.55), channel_id=1, source_target_pairs={{0,4},{4,8},{8,12},{12,16},{16,20},{20,24},{24,28},{1,5},{5,9},{9,... | collective-permute-start | bytes 491528 | tf_op jit(solution)/shard_map/ppermute | solution.py:18
  57.5 7.9 %collective-permute-start.7 = (f32[80,1,1,512]{3,2,0,1:T(1,128)S(1)}, f32[80,1,1,512]{3,2,0,1:T(1,128)S(1)}, u32[]{:S(2)}, u32[]{:S(2)}) collective-permute-start(f32[80,1,1,512]{3,2,0,1:T(1,128)S(1)} %get-tuple-element.56), channel_id=1, source_target_pairs={{4,0},{8,4},{12,8},{16,12},{20,16},{24,20},{28,24},{5,1},{9,5},{13... | collective-permute-start | bytes 491528 | tf_op jit(solution)/shard_map/ppermute | solution.py:19
  70.1 7.4 %collective-permute-start.8 = (f32[80,1,1,512]{3,2,0,1:T(1,128)S(1)}, f32[80,1,1,512]{3,2,0,1:T(1,128)S(1)}, u32[]{:S(2)}, u32[]{:S(2)}) collective-permute-start(f32[80,1,1,512]{3,2,0,1:T(1,128)S(1)} %get-tuple-element.45), channel_id=1, source_target_pairs={{0,4},{4,8},{8,12},{12,16},{16,20},{20,24},{24,28},{1,5},{5,9},{9,... | collective-permute-start | bytes 491528 | tf_op jit(solution)/shard_map/ppermute | solution.py:18
  74.7 7.9 %collective-permute-start.9 = (f32[80,1,1,512]{3,2,0,1:T(1,128)S(1)}, f32[80,1,1,512]{3,2,0,1:T(1,128)S(1)}, u32[]{:S(2)}, u32[]{:S(2)}) collective-permute-start(f32[80,1,1,512]{3,2,0,1:T(1,128)S(1)} %get-tuple-element.46), channel_id=1, source_target_pairs={{4,0},{8,4},{12,8},{16,12},{20,16},{24,20},{28,24},{5,1},{9,5},{13... | collective-permute-start | bytes 491528 | tf_op jit(solution)/shard_map/ppermute | solution.py:19
  83.5 7.4 %collective-permute-start.10 = (f32[80,1,1,512]{3,2,0,1:T(1,128)S(1)}, f32[80,1,1,512]{3,2,0,1:T(1,128)S(1)}, u32[]{:S(2)}, u32[]{:S(2)}) collective-permute-start(f32[80,1,1,512]{3,2,0,1:T(1,128)S(1)} %get-tuple-element.43), channel_id=1, source_target_pairs={{0,4},{4,8},{8,12},{12,16},{16,20},{20,24},{24,28},{1,5},{5,9},{9,... | collective-permute-start | bytes 491528 | tf_op jit(solution)/shard_map/ppermute | solution.py:18
  88.1 7.9 %collective-permute-start.11 = (f32[80,1,1,512]{3,2,0,1:T(1,128)S(1)}, f32[80,1,1,512]{3,2,0,1:T(1,128)S(1)}, u32[]{:S(2)}, u32[]{:S(2)}) collective-permute-start(f32[80,1,1,512]{3,2,0,1:T(1,128)S(1)} %get-tuple-element.44), channel_id=1, source_target_pairs={{4,0},{8,4},{12,8},{16,12},{20,16},{24,20},{28,24},{5,1},{9,5},{13... | collective-permute-start | bytes 491528 | tf_op jit(solution)/shard_map/ppermute | solution.py:19
  187.2 10.6 %collective-permute-start.12 = (f32[80,1,1,512]{3,2,0,1:T(1,128)S(1)}, f32[80,1,1,512]{3,2,0,1:T(1,128)S(1)}, u32[]{:S(2)}, u32[]{:S(2)}) collective-permute-start(f32[80,1,1,512]{3,2,0,1:T(1,128)S(1)} %get-tuple-element.33), channel_id=1, source_target_pairs={{0,4},{4,8},{8,12},{12,16},{16,20},{20,24},{24,28},{1,5},{5,9},{9,... | collective-permute-start | bytes 491528 | tf_op jit(solution)/shard_map/ppermute | solution.py:18
  191.4 7.2 %collective-permute-start.13 = (f32[80,1,1,512]{3,2,0,1:T(1,128)S(1)}, f32[80,1,1,512]{3,2,0,1:T(1,128)S(1)}, u32[]{:S(2)}, u32[]{:S(2)}) collective-permute-start(f32[80,1,1,512]{3,2,0,1:T(1,128)S(1)} %get-tuple-element.34), channel_id=1, source_target_pairs={{4,0},{8,4},{12,8},{16,12},{20,16},{24,20},{28,24},{5,1},{9,5},{13... | collective-permute-start | bytes 491528 | tf_op jit(solution)/shard_map/ppermute | solution.py:19
  199.6 6.4 %collective-permute-start.14 = (f32[80,1,1,512]{3,2,0,1:T(1,128)S(1)}, f32[80,1,1,512]{3,2,0,1:T(1,128)S(1)}, u32[]{:S(2)}, u32[]{:S(2)}) collective-permute-start(f32[80,1,1,512]{3,2,0,1:T(1,128)S(1)} %get-tuple-element.31), channel_id=1, source_target_pairs={{0,4},{4,8},{8,12},{12,16},{16,20},{20,24},{24,28},{1,5},{5,9},{9,... | collective-permute-start | bytes 491528 | tf_op jit(solution)/shard_map/ppermute | solution.py:18
  203.1 7.2 %collective-permute-start.15 = (f32[80,1,1,512]{3,2,0,1:T(1,128)S(1)}, f32[80,1,1,512]{3,2,0,1:T(1,128)S(1)}, u32[]{:S(2)}, u32[]{:S(2)}) collective-permute-start(f32[80,1,1,512]{3,2,0,1:T(1,128)S(1)} %get-tuple-element.32), channel_id=1, source_target_pairs={{4,0},{8,4},{12,8},{16,12},{20,16},{24,20},{28,24},{5,1},{9,5},{13... | collective-permute-start | bytes 491528 | tf_op jit(solution)/shard_map/ppermute | solution.py:19
  215.0 6.5 %collective-permute-start.16 = (f32[80,1,1,512]{3,2,0,1:T(1,128)S(1)}, f32[80,1,1,512]{3,2,0,1:T(1,128)S(1)}, u32[]{:S(2)}, u32[]{:S(2)}) collective-permute-start(f32[80,1,1,512]{3,2,0,1:T(1,128)S(1)} %get-tuple-element.21), channel_id=1, source_target_pairs={{0,4},{4,8},{8,12},{12,16},{16,20},{20,24},{24,28},{1,5},{5,9},{9,... | collective-permute-start | bytes 491528 | tf_op jit(solution)/shard_map/ppermute | solution.py:18
  218.8 7.2 %collective-permute-start.17 = (f32[80,1,1,512]{3,2,0,1:T(1,128)S(1)}, f32[80,1,1,512]{3,2,0,1:T(1,128)S(1)}, u32[]{:S(2)}, u32[]{:S(2)}) collective-permute-start(f32[80,1,1,512]{3,2,0,1:T(1,128)S(1)} %get-tuple-element.22), channel_id=1, source_target_pairs={{4,0},{8,4},{12,8},{16,12},{20,16},{24,20},{28,24},{5,1},{9,5},{13... | collective-permute-start | bytes 491528 | tf_op jit(solution)/shard_map/ppermute | solution.py:19
  227.0 7.2 %collective-permute-start.18 = (f32[80,1,1,512]{3,2,0,1:T(1,128)S(1)}, f32[80,1,1,512]{3,2,0,1:T(1,128)S(1)}, u32[]{:S(2)}, u32[]{:S(2)}) collective-permute-start(f32[80,1,1,512]{3,2,0,1:T(1,128)S(1)} %get-tuple-element.19), channel_id=1, source_target_pairs={{0,4},{4,8},{8,12},{12,16},{16,20},{20,24},{24,28},{1,5},{5,9},{9,... | collective-permute-start | bytes 491528 | tf_op jit(solution)/shard_map/ppermute | solution.py:18
  231.4 7.9 %collective-permute-start.19 = (f32[80,1,1,512]{3,2,0,1:T(1,128)S(1)}, f32[80,1,1,512]{3,2,0,1:T(1,128)S(1)}, u32[]{:S(2)}, u32[]{:S(2)}) collective-permute-start(f32[80,1,1,512]{3,2,0,1:T(1,128)S(1)} %get-tuple-element.20), channel_id=1, source_target_pairs={{4,0},{8,4},{12,8},{16,12},{20,16},{24,20},{28,24},{5,1},{9,5},{13... | collective-permute-start | bytes 491528 | tf_op jit(solution)/shard_map/ppermute | solution.py:19
  287.1 6.0 %copy-start = (bf16[20,4,2,512]{3,2,1,0:T(2,128)(2,1)S(1)}, bf16[20,4,2,512]{3,2,1,0:T(2,128)(2,1)}, u32[]{:S(2)}) copy-start(bf16[20,4,2,512]{3,2,1,0:T(2,128)(2,1)} %param.4) | copy-start | bytes 491524
  287.4 5.7 %copy-start.2 = (f32[2,512]{1,0:T(2,128)}, f32[2,512]{1,0:T(2,128)S(1)}, u32[]{:S(2)}) copy-start(f32[2,512]{1,0:T(2,128)S(1)} %multiply_reduce_fusion) | copy-start | bytes 12292
  (1 other events, 0.7 us)
where the time goes:
time: 295 us; the launch traced here: 294 us
  blocking collectives  131 us (44%)
  waiting for transfers between devices  64.3 us (22%)
  starting transfers between devices  59.9 us (20%)
  other arithmetic  23 us (8%)
  local copies, waits for them, and re-layouts  11.1 us (4%)
  between operations  5.15 us (2%)
    psum x2, blocking collectives, norm_of(): return lax.psum(jnp.sum(residual * residual), ('grid', 'mem'))  82.7 us
    ppermute x10, waiting for transfers between devices, padded(): after = lax.ppermute(leading, axis, down)  43.5 us
    ppermute x10, starting transfers between devices, padded(): before = lax.ppermute(last, axis, up)  42.3 us
    psum x1, blocking collectives, local(): step_size = norm_now / lax.psum(jnp.sum(direction * image), ('grid', 'mem'))  42.2 us
    ppermute x10, waiting for transfers between devices, padded(): before = lax.ppermute(last, axis, up)  18.5 us
    ppermute x10, starting transfers between devices, padded(): after = lax.ppermute(leading, axis, down)  13.3 us
    add x10, other arithmetic, smooth(): centre + diffusion * (extended[:, :, :-2] + extended[:, :, 2:] - 2.0 * ce...  7.27 us
    add x6, other arithmetic, smooth(): field + diffusion * (jnp.roll(field, 1, 3) + jnp.roll(field, -1, 3) - 2.0...  6.6 us
  transfers between devices with their start and end apart: 21, of which 21 were waited for; matrix products, arithmetic and copies ran while one was open for 1% of the time, Pallas kernels for 0%

commit v1 on v0

--- a/solution.py
+++ b/solution.py
@@ -43,7 +43,19 @@
 def local(members, innovation, observed_count, obs_precision):
     mem_index = lax.axis_index("mem")
     level_share = members.shape[1] // lax.axis_size("mem")
-    perturbed = lax.all_to_all(members, "mem", split_axis=1, concat_axis=0, tiled=True)
+    ways, here = (lax.axis_size("mem"), lax.axis_index("mem"))
+    width_2 = members.shape[1] // ways
+    shape = list(members.shape)
+    shape[1] = width_2
+    height = shape[0]
+    shape[0] = height * ways
+    full = jnp.zeros(shape, members.dtype)
+    for mask in range(ways):
+        part = lax.dynamic_slice_in_dim(members, (here ^ mask) * width_2, width_2, axis=1)
+        if mask:
+            part = lax.ppermute(part, "mem", [(d, d ^ mask) for d in range(ways)])
+        full = lax.dynamic_update_slice_in_dim(full, part, (here ^ mask) * height, axis=0)
+    perturbed = full
     precision = lax.dynamic_slice_in_dim(obs_precision, mem_index * level_share, level_share, 0)
     local_innovation = lax.dynamic_slice_in_dim(innovation, mem_index * level_share, level_share, 0)
     weight = observed_count.astype(jnp.float32)[None] * precision[:, None, None]

time: 295 us -> 292 us (0.990)
    all_to_all x1 -> x0, starting transfers between devices: 4.26 us -> none  [local(): lax.all_to_all(members, 'mem', split_axis=1, concat_axis=0, tiled=True)]
    ppermute x0 -> x3, starting transfers between devices: none -> 3.22 us  [local(): part = lax.ppermute(part, 'mem', [(d, d ^ mask) for d in range(ways)])]
  transfers between devices with their start and end apart: 21 -> 23, of which waited for: 21 -> 21; matrix products, arithmetic and copies ran while one was open for 1% -> 1% of each run, Pallas kernels for 0% -> 0%
where the time goes in v1:
time: 292 us; the launch traced here: 291 us
  blocking collectives  131 us (45%)
  waiting for transfers between devices  63.3 us (22%)
  starting transfers between devices  58.1 us (20%)
  other arithmetic  23.3 us (8%)
  local copies, waits for them, and re-layouts  9.84 us (3%)
  between operations  5.07 us (2%)
    psum x2, blocking collectives, norm_of(): return lax.psum(jnp.sum(residual * residual), ('grid', 'mem'))  83.5 us
    ppermute x10, waiting for transfers between devices, padded(): after = lax.ppermute(leading, axis, down)  43 us
    psum x1, blocking collectives, local(): step_size = norm_now / lax.psum(jnp.sum(direction * image), ('grid', 'mem'))  42.2 us
    ppermute x10, starting transfers between devices, padded(): before = lax.ppermute(last, axis, up)  41.6 us
    ppermute x10, waiting for transfers between devices, padded(): before = lax.ppermute(last, axis, up)  18.3 us
    ppermute x10, starting transfers between devices, padded(): after = lax.ppermute(leading, axis, down)  13.3 us
    add x10, other arithmetic, smooth(): centre + diffusion * (extended[:, :, :-2] + extended[:, :, 2:] - 2.0 * ce...  7.28 us
    add x6, other arithmetic, smooth(): field + diffusion * (jnp.roll(field, 1, 3) + jnp.roll(field, -1, 3) - 2.0...  6.59 us
  transfers between devices with their start and end apart: 23, of which 21 were waited for; matrix products, arithmetic and copies ran while one was open for 1% of the time, Pallas kernels for 0%

profile of v1, /device:TPU:0, one launch (start us, length us, event | category | flops | bytes accessed | tf_op | source)
XLA Modules:
  0.0 291.0 jit_solution(3940848991839391804)
XLA Ops:
  9.4 3.4 %collective-permute-start.3 = (f32[80,1,1,512]{3,2,1,0:T(1,128)S(1)}, f32[80,1,1,512]{3,2,1,0:T(1,128)S(1)}, u32[]{:S(2)}, u32[]{:S(2)}) collective-permute-start(f32[80,1,1,512]{3,2,1,0:T(1,128)S(1)} %get-tuple-element.69), channel_id=1, source_target_pairs={{0,4},{4,8},{8,12},{12,16},{16,20},{20,24},{24,28},{1,5},{5,9},{9,... | collective-permute-start | bytes 491528 | tf_op jit(solution)/shard_map/ppermute | solution.py:18
  15.6 4.4 %collective-permute-done.4 = f32[80,1,1,512]{3,2,1,0:T(1,128)S(1)} collective-permute-done((f32[80,1,1,512]{3,2,1,0:T(1,128)S(1)}, f32[80,1,1,512]{3,2,1,0:T(1,128)S(1)}, u32[]{:S(2)}, u32[]{:S(2)}) %collective-permute-start.4) | collective-permute-done | bytes 163872 | tf_op jit(solution)/shard_map/ppermute | solution.py:19
  21.0 4.4 %collective-permute-start.5 = (f32[80,1,1,512]{3,2,1,0:T(1,128)S(1)}, f32[80,1,1,512]{3,2,1,0:T(1,128)S(1)}, u32[]{:S(2)}, u32[]{:S(2)}) collective-permute-start(f32[80,1,1,512]{3,2,1,0:T(1,128)S(1)} %get-tuple-element.67), channel_id=1, source_target_pairs={{0,4},{4,8},{8,12},{12,16},{16,20},{20,24},{24,28},{1,5},{5,9},{9,... | collective-permute-start | bytes 491528 | tf_op jit(solution)/shard_map/ppermute | solution.py:18
  28.1 4.4 %collective-permute-done.6 = f32[80,1,1,512]{3,2,1,0:T(1,128)S(1)} collective-permute-done((f32[80,1,1,512]{3,2,1,0:T(1,128)S(1)}, f32[80,1,1,512]{3,2,1,0:T(1,128)S(1)}, u32[]{:S(2)}, u32[]{:S(2)}) %collective-permute-start.6) | collective-permute-done | bytes 163872 | tf_op jit(solution)/shard_map/ppermute | solution.py:19
  36.5 4.4 %collective-permute-start.7 = (f32[80,1,1,512]{3,2,1,0:T(1,128)S(1)}, f32[80,1,1,512]{3,2,1,0:T(1,128)S(1)}, u32[]{:S(2)}, u32[]{:S(2)}) collective-permute-start(f32[80,1,1,512]{3,2,1,0:T(1,128)S(1)} %get-tuple-element.57), channel_id=1, source_target_pairs={{0,4},{4,8},{8,12},{12,16},{16,20},{20,24},{24,28},{1,5},{5,9},{9,... | collective-permute-start | bytes 491528 | tf_op jit(solution)/shard_map/ppermute | solution.py:18
  43.7 4.5 %collective-permute-done.8 = f32[80,1,1,512]{3,2,1,0:T(1,128)S(1)} collective-permute-done((f32[80,1,1,512]{3,2,1,0:T(1,128)S(1)}, f32[80,1,1,512]{3,2,1,0:T(1,128)S(1)}, u32[]{:S(2)}, u32[]{:S(2)}) %collective-permute-start.8) | collective-permute-done | bytes 163872 | tf_op jit(solution)/shard_map/ppermute | solution.py:19
  49.2 4.5 %collective-permute-start.9 = (f32[80,1,1,512]{3,2,1,0:T(1,128)S(1)}, f32[80,1,1,512]{3,2,1,0:T(1,128)S(1)}, u32[]{:S(2)}, u32[]{:S(2)}) collective-permute-start(f32[80,1,1,512]{3,2,1,0:T(1,128)S(1)} %get-tuple-element.55), channel_id=1, source_target_pairs={{0,4},{4,8},{8,12},{12,16},{16,20},{20,24},{24,28},{1,5},{5,9},{9,... | collective-permute-start | bytes 491528 | tf_op jit(solution)/shard_map/ppermute | solution.py:18
  56.5 4.9 %collective-permute-done.10 = f32[80,1,1,512]{3,2,1,0:T(1,128)S(1)} collective-permute-done((f32[80,1,1,512]{3,2,1,0:T(1,128)S(1)}, f32[80,1,1,512]{3,2,1,0:T(1,128)S(1)}, u32[]{:S(2)}, u32[]{:S(2)}) %collective-permute-start.10) | collective-permute-done | bytes 163872 | tf_op jit(solution)/shard_map/ppermute | solution.py:19
  66.3 4.5 %collective-permute-start.11 = (f32[80,1,1,512]{3,2,1,0:T(1,128)S(1)}, f32[80,1,1,512]{3,2,1,0:T(1,128)S(1)}, u32[]{:S(2)}, u32[]{:S(2)}) collective-permute-start(f32[80,1,1,512]{3,2,1,0:T(1,128)S(1)} %get-tuple-element.45), channel_id=1, source_target_pairs={{0,4},{4,8},{8,12},{12,16},{16,20},{20,24},{24,28},{1,5},{5,9},{9,... | collective-permute-start | bytes 491528 | tf_op jit(solution)/shard_map/ppermute | solution.py:18
  73.6 5.2 %collective-permute-done.12 = f32[80,1,1,512]{3,2,1,0:T(1,128)S(1)} collective-permute-done((f32[80,1,1,512]{3,2,1,0:T(1,128)S(1)}, f32[80,1,1,512]{3,2,1,0:T(1,128)S(1)}, u32[]{:S(2)}, u32[]{:S(2)}) %collective-permute-start.12) | collective-permute-done | bytes 163872 | tf_op jit(solution)/shard_map/ppermute | solution.py:19
  79.9 4.5 %collective-permute-start.13 = (f32[80,1,1,512]{3,2,1,0:T(1,128)S(1)}, f32[80,1,1,512]{3,2,1,0:T(1,128)S(1)}, u32[]{:S(2)}, u32[]{:S(2)}) collective-permute-start(f32[80,1,1,512]{3,2,1,0:T(1,128)S(1)} %get-tuple-element.43), channel_id=1, source_target_pairs={{0,4},{4,8},{8,12},{12,16},{16,20},{20,24},{24,28},{1,5},{5,9},{9,... | collective-permute-start | bytes 491528 | tf_op jit(solution)/shard_map/ppermute | solution.py:18
  87.2 4.9 %collective-permute-done.14 = f32[80,1,1,512]{3,2,1,0:T(1,128)S(1)} collective-permute-done((f32[80,1,1,512]{3,2,1,0:T(1,128)S(1)}, f32[80,1,1,512]{3,2,1,0:T(1,128)S(1)}, u32[]{:S(2)}, u32[]{:S(2)}) %collective-permute-start.14) | collective-permute-done | bytes 163872 | tf_op jit(solution)/shard_map/ppermute | solution.py:19
  96.6 42.7 %all-reduce = (f32[]{:T(128)}, f32[]{:T(128)}) all-reduce(f32[]{:T(128)} %get-tuple-element.3, f32[]{:T(128)} %get-tuple-element.2), channel_id=1, replica_groups=mesh['grid'=8,'mem'=4] {'grid','mem'}, use_global_device_ids=true, to_apply=%region_1.2 | all-reduce | flops 2 | bytes 16 | tf_op jit(solution)/shard_map/psum | solution.py:40
  141.5 40.8 %psum.30 = f32[]{:T(128)} all-reduce(f32[]{:T(128)} %multiply_reduce_fusion), channel_id=1, replica_groups=mesh['grid'=8,'mem'=4] {'grid','mem'}, use_global_device_ids=true, to_apply=%region_6.7 | all-reduce | flops 1 | bytes 8 | tf_op jit(solution)/shard_map/psum | solution.py:40
  184.1 4.2 %collective-permute-start.15 = (f32[80,1,1,512]{3,2,1,0:T(1,128)S(1)}, f32[80,1,1,512]{3,2,1,0:T(1,128)S(1)}, u32[]{:S(2)}, u32[]{:S(2)}) collective-permute-start(f32[80,1,1,512]{3,2,1,0:T(1,128)S(1)} %get-tuple-element.33), channel_id=1, source_target_pairs={{0,4},{4,8},{8,12},{12,16},{16,20},{20,24},{24,28},{1,5},{5,9},{9,... | collective-permute-start | bytes 491528 | tf_op jit(solution)/shard_map/ppermute | solution.py:18
  189.6 5.1 %collective-permute-done.15 = f32[80,1,1,512]{3,2,1,0:T(1,128)S(1)} collective-permute-done((f32[80,1,1,512]{3,2,1,0:T(1,128)S(1)}, f32[80,1,1,512]{3,2,1,0:T(1,128)S(1)}, u32[]{:S(2)}, u32[]{:S(2)}) %collective-permute-start.15) | collective-permute-done | bytes 163872 | tf_op jit(solution)/shard_map/ppermute | solution.py:18
  196.5 3.5 %collective-permute-start.17 = (f32[80,1,1,512]{3,2,1,0:T(1,128)S(1)}, f32[80,1,1,512]{3,2,1,0:T(1,128)S(1)}, u32[]{:S(2)}, u32[]{:S(2)}) collective-permute-start(f32[80,1,1,512]{3,2,1,0:T(1,128)S(1)} %get-tuple-element.31), channel_id=1, source_target_pairs={{0,4},{4,8},{8,12},{12,16},{16,20},{20,24},{24,28},{1,5},{5,9},{9,... | collective-permute-start | bytes 491528 | tf_op jit(solution)/shard_map/ppermute | solution.py:18
  202.9 4.4 %collective-permute-done.18 = f32[80,1,1,512]{3,2,1,0:T(1,128)S(1)} collective-permute-done((f32[80,1,1,512]{3,2,1,0:T(1,128)S(1)}, f32[80,1,1,512]{3,2,1,0:T(1,128)S(1)}, u32[]{:S(2)}, u32[]{:S(2)}) %collective-permute-start.18) | collective-permute-done | bytes 163872 | tf_op jit(solution)/shard_map/ppermute | solution.py:19
  212.1 3.7 %collective-permute-start.19 = (f32[80,1,1,512]{3,2,1,0:T(1,128)S(1)}, f32[80,1,1,512]{3,2,1,0:T(1,128)S(1)}, u32[]{:S(2)}, u32[]{:S(2)}) collective-permute-start(f32[80,1,1,512]{3,2,1,0:T(1,128)S(1)} %get-tuple-element.21), channel_id=1, source_target_pairs={{0,4},{4,8},{8,12},{12,16},{16,20},{20,24},{24,28},{1,5},{5,9},{9,... | collective-permute-start | bytes 491528 | tf_op jit(solution)/shard_map/ppermute | solution.py:18
  218.6 4.4 %collective-permute-done.20 = f32[80,1,1,512]{3,2,1,0:T(1,128)S(1)} collective-permute-done((f32[80,1,1,512]{3,2,1,0:T(1,128)S(1)}, f32[80,1,1,512]{3,2,1,0:T(1,128)S(1)}, u32[]{:S(2)}, u32[]{:S(2)}) %collective-permute-start.20) | collective-permute-done | bytes 163872 | tf_op jit(solution)/shard_map/ppermute | solution.py:19
  224.0 4.4 %collective-permute-start.21 = (f32[80,1,1,512]{3,2,1,0:T(1,128)S(1)}, f32[80,1,1,512]{3,2,1,0:T(1,128)S(1)}, u32[]{:S(2)}, u32[]{:S(2)}) collective-permute-start(f32[80,1,1,512]{3,2,1,0:T(1,128)S(1)} %get-tuple-element.19), channel_id=1, source_target_pairs={{0,4},{4,8},{8,12},{12,16},{16,20},{20,24},{24,28},{1,5},{5,9},{9,... | collective-permute-start | bytes 491528 | tf_op jit(solution)/shard_map/ppermute | solution.py:18
  231.2 5.1 %collective-permute-done.22 = f32[80,1,1,512]{3,2,1,0:T(1,128)S(1)} collective-permute-done((f32[80,1,1,512]{3,2,1,0:T(1,128)S(1)}, f32[80,1,1,512]{3,2,1,0:T(1,128)S(1)}, u32[]{:S(2)}, u32[]{:S(2)}) %collective-permute-start.22) | collective-permute-done | bytes 163872 | tf_op jit(solution)/shard_map/ppermute | solution.py:19
  240.7 42.2 %psum.31 = f32[]{:T(128)} all-reduce(f32[]{:T(128)} %fusion), channel_id=1, replica_groups=mesh['grid'=8,'mem'=4] {'grid','mem'}, use_global_device_ids=true, to_apply=%region_9.10 | all-reduce | flops 1 | bytes 8 | tf_op jit(solution)/shard_map/psum | solution.py:72
  284.5 5.7 %all-gather.1 = f32[4,2,512]{2,1,0:T(2,128)S(1)} all-gather(f32[1,2,512]{2,1,0:T(2,128)S(1)} %bitcast.8), channel_id=2, replica_groups=mesh['grid'=8,'mem'=4] {'mem'}, dimensions={0}, use_global_device_ids=true | all-gather | bytes 20480 | tf_op jit(solution)/shard_map/all_gather | solution.py:80
  (100 shorter events, 65.8 us)
Async XLA Ops:
  1.7 7.2 %collective-permute-start.2 = (bf16[20,1,2,512]{3,2,1,0:T(2,128)(2,1)S(1)}, bf16[20,1,2,512]{3,2,1,0:T(2,128)(2,1)S(1)}, u32[]{:S(2)}, u32[]{:S(2)}) collective-permute-start(bf16[20,1,2,512]{3,2,1,0:T(2,128)(2,1)S(1)} %get-tuple-element.71), channel_id=1, source_target_pairs={{0,3},{1,2},{2,1},{3,0},{4,7},{5,6},{6,5},{7,4},{8,11},{9,10},{10,... | collective-permute-start | bytes 122888 | tf_op jit(solution)/shard_map/ppermute | solution.py:56
  4.2 2.6 collective-permute-start
  4.9 4.0 %collective-permute-start.1 = (bf16[20,1,2,512]{3,2,1,0:T(2,128)(2,1)S(1)}, bf16[20,1,2,512]{3,2,1,0:T(2,128)(2,1)S(1)}, u32[]{:S(2)}, u32[]{:S(2)}) collective-permute-start(bf16[20,1,2,512]{3,2,1,0:T(2,128)(2,1)S(1)} %get-tuple-element.74), channel_id=1, source_target_pairs={{0,2},{1,3},{2,0},{3,1},{4,6},{5,7},{6,4},{7,5},{8,10},{9,11},{10,... | collective-permute-start | bytes 122888 | tf_op jit(solution)/shard_map/ppermute | solution.py:56
  9.4 6.2 %collective-permute-start.3 = (f32[80,1,1,512]{3,2,1,0:T(1,128)S(1)}, f32[80,1,1,512]{3,2,1,0:T(1,128)S(1)}, u32[]{:S(2)}, u32[]{:S(2)}) collective-permute-start(f32[80,1,1,512]{3,2,1,0:T(1,128)S(1)} %get-tuple-element.69), channel_id=1, source_target_pairs={{0,4},{4,8},{8,12},{12,16},{16,20},{20,24},{24,28},{1,5},{5,9},{9,... | collective-permute-start | bytes 491528 | tf_op jit(solution)/shard_map/ppermute | solution.py:18
  12.8 7.2 %collective-permute-start.4 = (f32[80,1,1,512]{3,2,1,0:T(1,128)S(1)}, f32[80,1,1,512]{3,2,1,0:T(1,128)S(1)}, u32[]{:S(2)}, u32[]{:S(2)}) collective-permute-start(f32[80,1,1,512]{3,2,1,0:T(1,128)S(1)} %get-tuple-element.70), channel_id=1, source_target_pairs={{4,0},{8,4},{12,8},{16,12},{20,16},{24,20},{28,24},{5,1},{9,5},{13... | collective-permute-start | bytes 491528 | tf_op jit(solution)/shard_map/ppermute | solution.py:19
  21.0 7.2 %collective-permute-start.5 = (f32[80,1,1,512]{3,2,1,0:T(1,128)S(1)}, f32[80,1,1,512]{3,2,1,0:T(1,128)S(1)}, u32[]{:S(2)}, u32[]{:S(2)}) collective-permute-start(f32[80,1,1,512]{3,2,1,0:T(1,128)S(1)} %get-tuple-element.67), channel_id=1, source_target_pairs={{0,4},{4,8},{8,12},{12,16},{16,20},{20,24},{24,28},{1,5},{5,9},{9,... | collective-permute-start | bytes 491528 | tf_op jit(solution)/shard_map/ppermute | solution.py:18
  25.3 7.2 %collective-permute-start.6 = (f32[80,1,1,512]{3,2,1,0:T(1,128)S(1)}, f32[80,1,1,512]{3,2,1,0:T(1,128)S(1)}, u32[]{:S(2)}, u32[]{:S(2)}) collective-permute-start(f32[80,1,1,512]{3,2,1,0:T(1,128)S(1)} %get-tuple-element.68), channel_id=1, source_target_pairs={{4,0},{8,4},{12,8},{16,12},{20,16},{24,20},{28,24},{5,1},{9,5},{13... | collective-permute-start | bytes 491528 | tf_op jit(solution)/shard_map/ppermute | solution.py:19
  36.5 7.2 %collective-permute-start.7 = (f32[80,1,1,512]{3,2,1,0:T(1,128)S(1)}, f32[80,1,1,512]{3,2,1,0:T(1,128)S(1)}, u32[]{:S(2)}, u32[]{:S(2)}) collective-permute-start(f32[80,1,1,512]{3,2,1,0:T(1,128)S(1)} %get-tuple-element.57), channel_id=1, source_target_pairs={{0,4},{4,8},{8,12},{12,16},{16,20},{20,24},{24,28},{1,5},{5,9},{9,... | collective-permute-start | bytes 491528 | tf_op jit(solution)/shard_map/ppermute | solution.py:18
  40.9 7.3 %collective-permute-start.8 = (f32[80,1,1,512]{3,2,1,0:T(1,128)S(1)}, f32[80,1,1,512]{3,2,1,0:T(1,128)S(1)}, u32[]{:S(2)}, u32[]{:S(2)}) collective-permute-start(f32[80,1,1,512]{3,2,1,0:T(1,128)S(1)} %get-tuple-element.58), channel_id=1, source_target_pairs={{4,0},{8,4},{12,8},{16,12},{20,16},{24,20},{28,24},{5,1},{9,5},{13... | collective-permute-start | bytes 491528 | tf_op jit(solution)/shard_map/ppermute | solution.py:19
  49.2 7.4 %collective-permute-start.9 = (f32[80,1,1,512]{3,2,1,0:T(1,128)S(1)}, f32[80,1,1,512]{3,2,1,0:T(1,128)S(1)}, u32[]{:S(2)}, u32[]{:S(2)}) collective-permute-start(f32[80,1,1,512]{3,2,1,0:T(1,128)S(1)} %get-tuple-element.55), channel_id=1, source_target_pairs={{0,4},{4,8},{8,12},{12,16},{16,20},{20,24},{24,28},{1,5},{5,9},{9,... | collective-permute-start | bytes 491528 | tf_op jit(solution)/shard_map/ppermute | solution.py:18
  53.7 7.7 %collective-permute-start.10 = (f32[80,1,1,512]{3,2,1,0:T(1,128)S(1)}, f32[80,1,1,512]{3,2,1,0:T(1,128)S(1)}, u32[]{:S(2)}, u32[]{:S(2)}) collective-permute-start(f32[80,1,1,512]{3,2,1,0:T(1,128)S(1)} %get-tuple-element.56), channel_id=1, source_target_pairs={{4,0},{8,4},{12,8},{16,12},{20,16},{24,20},{28,24},{5,1},{9,5},{13... | collective-permute-start | bytes 491528 | tf_op jit(solution)/shard_map/ppermute | solution.py:19
  66.3 7.4 %collective-permute-start.11 = (f32[80,1,1,512]{3,2,1,0:T(1,128)S(1)}, f32[80,1,1,512]{3,2,1,0:T(1,128)S(1)}, u32[]{:S(2)}, u32[]{:S(2)}) collective-permute-start(f32[80,1,1,512]{3,2,1,0:T(1,128)S(1)} %get-tuple-element.45), channel_id=1, source_target_pairs={{0,4},{4,8},{8,12},{12,16},{16,20},{20,24},{24,28},{1,5},{5,9},{9,... | collective-permute-start | bytes 491528 | tf_op jit(solution)/shard_map/ppermute | solution.py:18
  70.8 8.1 %collective-permute-start.12 = (f32[80,1,1,512]{3,2,1,0:T(1,128)S(1)}, f32[80,1,1,512]{3,2,1,0:T(1,128)S(1)}, u32[]{:S(2)}, u32[]{:S(2)}) collective-permute-start(f32[80,1,1,512]{3,2,1,0:T(1,128)S(1)} %get-tuple-element.46), channel_id=1, source_target_pairs={{4,0},{8,4},{12,8},{16,12},{20,16},{24,20},{28,24},{5,1},{9,5},{13... | collective-permute-start | bytes 491528 | tf_op jit(solution)/shard_map/ppermute | solution.py:19
  79.9 7.4 %collective-permute-start.13 = (f32[80,1,1,512]{3,2,1,0:T(1,128)S(1)}, f32[80,1,1,512]{3,2,1,0:T(1,128)S(1)}, u32[]{:S(2)}, u32[]{:S(2)}) collective-permute-start(f32[80,1,1,512]{3,2,1,0:T(1,128)S(1)} %get-tuple-element.43), channel_id=1, source_target_pairs={{0,4},{4,8},{8,12},{12,16},{16,20},{20,24},{24,28},{1,5},{5,9},{9,... | collective-permute-start | bytes 491528 | tf_op jit(solution)/shard_map/ppermute | solution.py:18
  84.4 7.7 %collective-permute-start.14 = (f32[80,1,1,512]{3,2,1,0:T(1,128)S(1)}, f32[80,1,1,512]{3,2,1,0:T(1,128)S(1)}, u32[]{:S(2)}, u32[]{:S(2)}) collective-permute-start(f32[80,1,1,512]{3,2,1,0:T(1,128)S(1)} %get-tuple-element.44), channel_id=1, source_target_pairs={{4,0},{8,4},{12,8},{16,12},{20,16},{24,20},{28,24},{5,1},{9,5},{13... | collective-permute-start | bytes 491528 | tf_op jit(solution)/shard_map/ppermute | solution.py:19
  184.1 10.6 %collective-permute-start.15 = (f32[80,1,1,512]{3,2,1,0:T(1,128)S(1)}, f32[80,1,1,512]{3,2,1,0:T(1,128)S(1)}, u32[]{:S(2)}, u32[]{:S(2)}) collective-permute-start(f32[80,1,1,512]{3,2,1,0:T(1,128)S(1)} %get-tuple-element.33), channel_id=1, source_target_pairs={{0,4},{4,8},{8,12},{12,16},{16,20},{20,24},{24,28},{1,5},{5,9},{9,... | collective-permute-start | bytes 491528 | tf_op jit(solution)/shard_map/ppermute | solution.py:18
  188.3 7.2 %collective-permute-start.16 = (f32[80,1,1,512]{3,2,1,0:T(1,128)S(1)}, f32[80,1,1,512]{3,2,1,0:T(1,128)S(1)}, u32[]{:S(2)}, u32[]{:S(2)}) collective-permute-start(f32[80,1,1,512]{3,2,1,0:T(1,128)S(1)} %get-tuple-element.34), channel_id=1, source_target_pairs={{4,0},{8,4},{12,8},{16,12},{20,16},{24,20},{28,24},{5,1},{9,5},{13... | collective-permute-start | bytes 491528 | tf_op jit(solution)/shard_map/ppermute | solution.py:19
  196.5 6.4 %collective-permute-start.17 = (f32[80,1,1,512]{3,2,1,0:T(1,128)S(1)}, f32[80,1,1,512]{3,2,1,0:T(1,128)S(1)}, u32[]{:S(2)}, u32[]{:S(2)}) collective-permute-start(f32[80,1,1,512]{3,2,1,0:T(1,128)S(1)} %get-tuple-element.31), channel_id=1, source_target_pairs={{0,4},{4,8},{8,12},{12,16},{16,20},{20,24},{24,28},{1,5},{5,9},{9,... | collective-permute-start | bytes 491528 | tf_op jit(solution)/shard_map/ppermute | solution.py:18
  200.1 7.2 %collective-permute-start.18 = (f32[80,1,1,512]{3,2,1,0:T(1,128)S(1)}, f32[80,1,1,512]{3,2,1,0:T(1,128)S(1)}, u32[]{:S(2)}, u32[]{:S(2)}) collective-permute-start(f32[80,1,1,512]{3,2,1,0:T(1,128)S(1)} %get-tuple-element.32), channel_id=1, source_target_pairs={{4,0},{8,4},{12,8},{16,12},{20,16},{24,20},{28,24},{5,1},{9,5},{13... | collective-permute-start | bytes 491528 | tf_op jit(solution)/shard_map/ppermute | solution.py:19
  212.1 6.5 %collective-permute-start.19 = (f32[80,1,1,512]{3,2,1,0:T(1,128)S(1)}, f32[80,1,1,512]{3,2,1,0:T(1,128)S(1)}, u32[]{:S(2)}, u32[]{:S(2)}) collective-permute-start(f32[80,1,1,512]{3,2,1,0:T(1,128)S(1)} %get-tuple-element.21), channel_id=1, source_target_pairs={{0,4},{4,8},{8,12},{12,16},{16,20},{20,24},{24,28},{1,5},{5,9},{9,... | collective-permute-start | bytes 491528 | tf_op jit(solution)/shard_map/ppermute | solution.py:18
  215.8 7.2 %collective-permute-start.20 = (f32[80,1,1,512]{3,2,1,0:T(1,128)S(1)}, f32[80,1,1,512]{3,2,1,0:T(1,128)S(1)}, u32[]{:S(2)}, u32[]{:S(2)}) collective-permute-start(f32[80,1,1,512]{3,2,1,0:T(1,128)S(1)} %get-tuple-element.22), channel_id=1, source_target_pairs={{4,0},{8,4},{12,8},{16,12},{20,16},{24,20},{28,24},{5,1},{9,5},{13... | collective-permute-start | bytes 491528 | tf_op jit(solution)/shard_map/ppermute | solution.py:19
  224.0 7.2 %collective-permute-start.21 = (f32[80,1,1,512]{3,2,1,0:T(1,128)S(1)}, f32[80,1,1,512]{3,2,1,0:T(1,128)S(1)}, u32[]{:S(2)}, u32[]{:S(2)}) collective-permute-start(f32[80,1,1,512]{3,2,1,0:T(1,128)S(1)} %get-tuple-element.19), channel_id=1, source_target_pairs={{0,4},{4,8},{8,12},{12,16},{16,20},{20,24},{24,28},{1,5},{5,9},{9,... | collective-permute-start | bytes 491528 | tf_op jit(solution)/shard_map/ppermute | solution.py:18
  228.4 7.9 %collective-permute-start.22 = (f32[80,1,1,512]{3,2,1,0:T(1,128)S(1)}, f32[80,1,1,512]{3,2,1,0:T(1,128)S(1)}, u32[]{:S(2)}, u32[]{:S(2)}) collective-permute-start(f32[80,1,1,512]{3,2,1,0:T(1,128)S(1)} %get-tuple-element.20), channel_id=1, source_target_pairs={{4,0},{8,4},{12,8},{16,12},{20,16},{24,20},{28,24},{5,1},{9,5},{13... | collective-permute-start | bytes 491528 | tf_op jit(solution)/shard_map/ppermute | solution.py:19
  284.5 5.8 %copy-start.2 = (f32[2,512]{1,0:T(2,128)}, f32[2,512]{1,0:T(2,128)S(1)}, u32[]{:S(2)}) copy-start(f32[2,512]{1,0:T(2,128)S(1)} %fusion.3) | copy-start | bytes 12292
  (3 other events, 8.1 us)
